TPU v7x, 128 devices: a whole 4x4x4 slice. The times are simulated.
128 devices in a mesh: xb: 16 (over y, z), yb: 8 (over x, core).
Axes of the slice: x: 4, y: 4, z: 4, core: 2. Of those that a mesh axis runs over, the one named last changes fastest.
Arguments:
- initial_guess: float32 [128, 512, 256], P('xb', 'yb'), may hold values from -4 to 4
- right_side: float32 [128, 512, 256], P('xb', 'yb'), may hold values from -8 to 8
- coefficient: float32 [128, 512, 256], P('xb', 'yb'), may hold values from 0.3 to 3
Outputs:
- fine_field: float32 [128, 512, 256], P('xb', 'yb')
- middle_field: float32 [64, 256, 128], P('xb', 'yb')
- lower_field: float32 [32, 128, 64], P('xb', 'yb')
- coarse_field: float32 [16, 64, 32], P('xb', 'yb')
All inputs are finite; a program needn't handle non-finite values.
Results may differ from a plain program's by a relative error of at most 0.00002.
Values sent between devices are 32-bit elements; how exact they have to be, the bound alone decides.
No kernel may reach another device: no remote copies, remote signals or barrier semaphores. Data moves between devices by JAX's collectives and lax.ppermute only.
A program may use at most 192 MiB of HBM per device.

v0:
```python
import jax
import jax.numpy as jnp
from jax import lax
from jax.sharding import PartitionSpec as P

COARSE_ITERS = 8
damping_alpha = 0.05
cheb_theta = 1.15
cheb_delta = 0.85
cheb_sigma = cheb_theta / cheb_delta
cheb_first = 1.0 / cheb_sigma
cheb_second = 1.0 / (2.0 * cheb_sigma - cheb_first)
cheb_carry = cheb_second * cheb_first
cheb_resid = 2.0 * cheb_second / cheb_delta
jacobi_weight = 0.8


def with_halo(block, sides, width):
    for axis, dim in sides:
        count = lax.axis_size(axis)
        forward = [(i, i + 1) for i in range(count - 1)]
        backward = [(target, source) for source, target in forward]
        low = lax.ppermute(
            lax.slice_in_dim(block, block.shape[dim] - width, None, axis=dim), axis, forward
        )
        high = lax.ppermute(lax.slice_in_dim(block, 0, width, axis=dim), axis, backward)
        block = jnp.concatenate([low, block, high], axis=dim)
    return block


def neighbours(padded):
    return [
        padded[2:, 1:-1, 1:-1],
        padded[:-2, 1:-1, 1:-1],
        padded[1:-1, 2:, 1:-1],
        padded[1:-1, :-2, 1:-1],
        padded[1:-1, 1:-1, 2:],
        padded[1:-1, 1:-1, :-2],
    ]


def face_weights(padded_coef, scale):
    centre = padded_coef[1:-1, 1:-1, 1:-1]
    weights = [0.5 * scale * (centre + other) for other in neighbours(padded_coef)]
    diagonal = damping_alpha + weights[0]
    for other in weights[1:]:
        diagonal = diagonal + other
    return (weights, diagonal)


def apply_operator(padded, field, weights, diagonal):
    result = diagonal * field
    for weight, other in zip(weights, neighbours(padded)):
        result = result - weight * other
    return result


def smooth_level(start, right_side, coefficient, scale, extend, padded_coef=None):
    padded_coef = extend(coefficient)
    weights, diagonal = face_weights(padded_coef, scale)
    if start is None:
        start = jnp.zeros_like(right_side)
        residual = right_side
    else:
        residual = right_side - apply_operator(extend(start), start, weights, diagonal)
    first_step = residual / (cheb_theta * diagonal)
    first = start + first_step
    residual = right_side - apply_operator(extend(first), first, weights, diagonal)
    second_step = cheb_carry * first_step + cheb_resid * residual / diagonal
    second = first + second_step
    residual = right_side - apply_operator(extend(second), second, weights, diagonal)
    return (second, residual)


def pair_matrix(count):
    rows = jnp.arange(count // 2)[:, None]
    cols = jnp.arange(count)[None, :] // 2
    return (rows == cols).astype(jnp.float32)


def restrict_field(field):
    sx, sy, sz = field.shape
    halves = field.reshape(sx // 2, 2, sy, sz)
    summed = halves[:, 0] + halves[:, 1]
    summed = jnp.einsum("xyZ,zZ->xyz", summed, pair_matrix(sz), precision=lax.Precision.HIGHEST)
    pairs_y = jnp.broadcast_to(pair_matrix(sy), (sx // 2, sy // 2, sy))
    summed = jnp.einsum("xyY,xYz->xyz", pairs_y, summed, precision=lax.Precision.HIGHEST)
    return summed * 0.125


def coarse_solve(right_side, coefficient, scale, extend):
    weights, diagonal = face_weights(extend(coefficient), scale)
    field = jnp.zeros_like(right_side)
    for repeat in range(COARSE_ITERS):
        field = (
            field
            + jacobi_weight
            * (right_side - apply_operator(extend(field), field, weights, diagonal))
            / diagonal
        )
    leftover = right_side - apply_operator(extend(field), field, weights, diagonal)
    ones_field = jnp.ones_like(right_side)
    image_ones = apply_operator(extend(ones_field), ones_field, weights, diagonal)
    return field + jnp.sum(leftover) / jnp.sum(image_ones)


def extend_all(field):
    return jnp.pad(field, 1)


def extend_local(field):
    padded = with_halo(field, (("xb", 0), ("yb", 1)), 1)
    return jnp.pad(padded, ((0, 0), (0, 0), (1, 1)))


def collect_grid(right_side, coefficient):
    sx, sy, sz = right_side.shape
    count_x = lax.axis_size("xb")
    count_y = lax.axis_size("yb")
    flat = (
        lax.all_gather(right_side.reshape(1, -1), ("xb", "yb"), axis=0, tiled=True),
        lax.all_gather(coefficient.reshape(1, -1), ("xb", "yb"), axis=0, tiled=True),
    )
    return tuple(
        (
            piece.reshape(count_x, count_y, sx, sy, sz)
            .transpose(0, 2, 1, 3, 4)
            .reshape(count_x * sx, count_y * sy, sz)
            for piece in flat
        )
    )


def own_block(whole, shape):
    start_x = lax.axis_index("xb") * shape[0]
    start_y = lax.axis_index("yb") * shape[1]
    return lax.dynamic_slice(whole, (start_x, start_y, jnp.int32(0)), shape)


def per_device(initial_guess, right_side, coefficient):
    fine, fine_res = smooth_level(initial_guess, right_side, coefficient, 1.0, extend_local, None)
    mid_coef = restrict_field(coefficient)
    middle, mid_res = smooth_level(
        None, restrict_field(fine_res), mid_coef, 0.25, extend_local, None
    )
    low_coef = restrict_field(mid_coef)
    low_rhs = restrict_field(mid_res)
    lower, low_res = smooth_level(None, low_rhs, low_coef, 0.0625, extend_local, None)
    coarse_rhs, coarse_coef = collect_grid(restrict_field(low_res), restrict_field(low_coef))
    coarse_whole = coarse_solve(coarse_rhs, coarse_coef, 0.015625, extend_all)
    sx, sy, sz = right_side.shape
    coarse = own_block(coarse_whole, (sx // 8, sy // 8, sz // 8))
    return (fine, middle, lower, coarse)


def solution(mesh):
    placed = (P("xb", "yb", None), P("xb", "yb", None), P("xb", "yb", None))
    return jax.shard_map(
        per_device,
        mesh=mesh,
        in_specs=placed,
        out_specs=(
            P("xb", "yb", None),
            P("xb", "yb", None),
            P("xb", "yb", None),
            P("xb", "yb", None),
        ),
        check_vma=False,
    )
```

profile of v0, /device:TPU:1, one launch (start us, length us, event | category | flops | bytes accessed | tf_op | source)
XLA Modules:
  0.0 239.6 jit_solution(1692704037954307134)
XLA Ops:
  0.6 0.9 fusion.348
  1.6 4.4 %collective-permute-start.1 = (f32[1,64,256]{2,1,0:T(8,128)S(1)}, f32[1,64,256]{2,1,0:T(8,128)S(1)}, u32[]{:S(2)}, u32[]{:S(2)}) collective-permute-start(f32[1,64,256]{2,1,0:T(8,128)S(1)} %get-tuple-element.31), channel_id=1, source_target_pairs={{0,8},{8,16},{16,24},{24,32},{32,40},{40,48},{48,56},{56,64},{64,7... | collective-permute-start | bytes 196616 | tf_op jit(solution)/shard_map/ppermute | solution.py:23
  6.0 1.3 collective-permute-start
  7.3 0.9 fusion.349
  8.1 4.2 %collective-permute-start.5 = (f32[1,64,256]{2,1,0:T(8,128)S(1)}, f32[1,64,256]{2,1,0:T(8,128)S(1)}, u32[]{:S(2)}, u32[]{:S(2)}) collective-permute-start(f32[1,64,256]{2,1,0:T(8,128)S(1)} %get-tuple-element.33), channel_id=1, source_target_pairs={{0,8},{8,16},{16,24},{24,32},{32,40},{40,48},{48,56},{56,64},{64,7... | collective-permute-start | bytes 196616 | tf_op jit(solution)/shard_map/ppermute | solution.py:23
  12.3 1.3 collective-permute-start.4
  13.7 1.4 fusion.217
  15.3 1.3 collective-permute-start.16
  16.8 4.6 %collective-permute-start.17 = (f32[1,32,128]{2,1,0:T(8,128)S(1)}, f32[1,32,128]{2,1,0:T(8,128)S(1)}, u32[]{:S(2)}, u32[]{:S(2)}) collective-permute-start(f32[1,32,128]{2,1,0:T(8,128)S(1)} %get-tuple-element.44), channel_id=1, source_target_pairs={{0,8},{8,16},{16,24},{24,32},{32,40},{40,48},{48,56},{56,64},{64,7... | collective-permute-start | bytes 49160 | tf_op jit(solution)/shard_map/ppermute | solution.py:23
  21.5 3.8 %collective-permute-start.2 = (f32[10,1,256]{2,1,0:T(1,128)S(1)}, f32[10,1,256]{2,1,0:T(1,128)S(1)}, u32[]{:S(2)}, u32[]{:S(2)}) collective-permute-start(f32[10,1,256]{2,1,0:T(1,128)S(1)} %get-tuple-element.23), channel_id=1, source_target_pairs={{1,0},{2,1},{3,2},{4,3},{5,4},{6,5},{7,6},{9,8},{10,9},{11,10},{12... | collective-permute-start | bytes 30728 | tf_op jit(solution)/shard_map/ppermute | solution.py:26
  25.4 3.0 %collective-permute-start.3 = (f32[10,1,256]{2,1,0:T(1,128)S(1)}, f32[10,1,256]{2,1,0:T(1,128)S(1)}, u32[]{:S(2)}, u32[]{:S(2)}) collective-permute-start(f32[10,1,256]{2,1,0:T(1,128)S(1)} %get-tuple-element.22), channel_id=1, source_target_pairs={{0,1},{1,2},{2,3},{3,4},{4,5},{5,6},{6,7},{8,9},{9,10},{10,11},{11... | collective-permute-start | bytes 30728 | tf_op jit(solution)/shard_map/ppermute | solution.py:23
  28.5 1.9 collective-permute-start.6
  30.4 3.6 %collective-permute-start.7 = (f32[10,1,256]{2,1,0:T(1,128)S(1)}, f32[10,1,256]{2,1,0:T(1,128)S(1)}, u32[]{:S(2)}, u32[]{:S(2)}) collective-permute-start(f32[10,1,256]{2,1,0:T(1,128)S(1)} %get-tuple-element.24), channel_id=1, source_target_pairs={{0,1},{1,2},{2,3},{3,4},{4,5},{5,6},{6,7},{8,9},{9,10},{10,11},{11... | collective-permute-start | bytes 30728 | tf_op jit(solution)/shard_map/ppermute | solution.py:23
  35.6 1.2 fusion.342
  36.8 1.3 collective-permute-start.8
  38.1 4.3 %collective-permute-start.9 = (f32[1,64,256]{2,1,0:T(8,128)S(1)}, f32[1,64,256]{2,1,0:T(8,128)S(1)}, u32[]{:S(2)}, u32[]{:S(2)}) collective-permute-start(f32[1,64,256]{2,1,0:T(8,128)S(1)} %get-tuple-element.28), channel_id=1, source_target_pairs={{0,8},{8,16},{16,24},{24,32},{32,40},{40,48},{48,56},{56,64},{64,7... | collective-permute-start | bytes 196616 | tf_op jit(solution)/shard_map/ppermute | solution.py:23
  42.4 1.3 collective-permute-done.9
  43.7 1.9 collective-permute-start.10
  45.7 4.8 %collective-permute-start.11 = (f32[10,1,256]{2,1,0:T(1,128)S(1)}, f32[10,1,256]{2,1,0:T(1,128)S(1)}, u32[]{:S(2)}, u32[]{:S(2)}) collective-permute-start(f32[10,1,256]{2,1,0:T(1,128)S(1)} %get-tuple-element.20), channel_id=1, source_target_pairs={{0,1},{1,2},{2,3},{3,4},{4,5},{5,6},{6,7},{8,9},{9,10},{10,11},{11... | collective-permute-start | bytes 30728 | tf_op jit(solution)/shard_map/ppermute | solution.py:23
  50.6 0.6 collective-permute-done.11
  51.7 1.2 fusion.181
  53.0 1.3 collective-permute-start.12
  54.3 4.6 %collective-permute-start.13 = (f32[1,64,256]{2,1,0:T(8,128)S(1)}, f32[1,64,256]{2,1,0:T(8,128)S(1)}, u32[]{:S(2)}, u32[]{:S(2)}) collective-permute-start(f32[1,64,256]{2,1,0:T(8,128)S(1)} %get-tuple-element.26), channel_id=1, source_target_pairs={{0,8},{8,16},{16,24},{24,32},{32,40},{40,48},{48,56},{56,64},{64,7... | collective-permute-start | bytes 196616 | tf_op jit(solution)/shard_map/ppermute | solution.py:23
  58.9 1.9 collective-permute-start.18
  60.9 4.5 %collective-permute-start.19 = (f32[6,1,128]{2,1,0:T(1,128)S(1)}, f32[6,1,128]{2,1,0:T(1,128)S(1)}, u32[]{:S(2)}, u32[]{:S(2)}) collective-permute-start(f32[6,1,128]{2,1,0:T(1,128)S(1)} %get-tuple-element.38), channel_id=1, source_target_pairs={{0,1},{1,2},{2,3},{3,4},{4,5},{5,6},{6,7},{8,9},{9,10},{10,11},{11... | collective-permute-start | bytes 9224 | tf_op jit(solution)/shard_map/ppermute | solution.py:23
  65.4 1.9 collective-permute-start.14
  67.3 3.6 %collective-permute-start.15 = (f32[10,1,256]{2,1,0:T(1,128)S(1)}, f32[10,1,256]{2,1,0:T(1,128)S(1)}, u32[]{:S(2)}, u32[]{:S(2)}) collective-permute-start(f32[10,1,256]{2,1,0:T(1,128)S(1)} %get-tuple-element.18), channel_id=1, source_target_pairs={{0,1},{1,2},{2,3},{3,4},{4,5},{5,6},{6,7},{8,9},{9,10},{10,11},{11... | collective-permute-start | bytes 30728 | tf_op jit(solution)/shard_map/ppermute | solution.py:23
  72.2 1.1 fusion.166
  73.9 1.3 collective-permute-start.20
  75.2 5.8 %collective-permute-start.21 = (f32[1,32,128]{2,1,0:T(8,128)S(1)}, f32[1,32,128]{2,1,0:T(8,128)S(1)}, u32[]{:S(2)}, u32[]{:S(2)}) collective-permute-start(f32[1,32,128]{2,1,0:T(8,128)S(1)} %get-tuple-element.42), channel_id=1, source_target_pairs={{0,8},{8,16},{16,24},{24,32},{32,40},{40,48},{48,56},{56,64},{64,7... | collective-permute-start | bytes 49160 | tf_op jit(solution)/shard_map/ppermute | solution.py:23
  81.1 1.3 collective-permute-start.28
  82.4 6.4 %collective-permute-start.29 = (f32[1,16,64]{2,1,0:T(8,128)S(1)}, f32[1,16,64]{2,1,0:T(8,128)S(1)}, u32[]{:S(2)}, u32[]{:S(2)}) collective-permute-start(f32[1,16,64]{2,1,0:T(8,128)S(1)} %get-tuple-element.56), channel_id=1, source_target_pairs={{0,8},{8,16},{16,24},{24,32},{32,40},{40,48},{48,56},{56,64},{64,7... | collective-permute-start | bytes 12296 | tf_op jit(solution)/shard_map/ppermute | solution.py:23
  88.8 1.9 collective-permute-start.22
  90.7 4.8 %collective-permute-start.23 = (f32[6,1,128]{2,1,0:T(1,128)S(1)}, f32[6,1,128]{2,1,0:T(1,128)S(1)}, u32[]{:S(2)}, u32[]{:S(2)}) collective-permute-start(f32[6,1,128]{2,1,0:T(1,128)S(1)} %get-tuple-element.36), channel_id=1, source_target_pairs={{0,1},{1,2},{2,3},{3,4},{4,5},{5,6},{6,7},{8,9},{9,10},{10,11},{11... | collective-permute-start | bytes 9224 | tf_op jit(solution)/shard_map/ppermute | solution.py:23
  95.6 0.6 collective-permute-done.23
  96.6 1.3 collective-permute-start.24
  97.9 6.7 %collective-permute-start.25 = (f32[1,32,128]{2,1,0:T(8,128)S(1)}, f32[1,32,128]{2,1,0:T(8,128)S(1)}, u32[]{:S(2)}, u32[]{:S(2)}) collective-permute-start(f32[1,32,128]{2,1,0:T(8,128)S(1)} %get-tuple-element.40), channel_id=1, source_target_pairs={{0,8},{8,16},{16,24},{24,32},{32,40},{40,48},{48,56},{56,64},{64,7... | collective-permute-start | bytes 49160 | tf_op jit(solution)/shard_map/ppermute | solution.py:23
  104.6 1.9 collective-permute-start.30
  106.6 4.5 %collective-permute-start.31 = (f32[4,1,64]{2,1,0:T(1,128)S(1)}, f32[4,1,64]{2,1,0:T(1,128)S(1)}, u32[]{:S(2)}, u32[]{:S(2)}) collective-permute-start(f32[4,1,64]{2,1,0:T(1,128)S(1)} %get-tuple-element.50), channel_id=1, source_target_pairs={{0,1},{1,2},{2,3},{3,4},{4,5},{5,6},{6,7},{8,9},{9,10},{10,11},{11... | collective-permute-start | bytes 3080 | tf_op jit(solution)/shard_map/ppermute | solution.py:23
  111.1 1.9 collective-permute-start.26
  113.0 3.6 %collective-permute-start.27 = (f32[6,1,128]{2,1,0:T(1,128)S(1)}, f32[6,1,128]{2,1,0:T(1,128)S(1)}, u32[]{:S(2)}, u32[]{:S(2)}) collective-permute-start(f32[6,1,128]{2,1,0:T(1,128)S(1)} %get-tuple-element.34), channel_id=1, source_target_pairs={{0,1},{1,2},{2,3},{3,4},{4,5},{5,6},{6,7},{8,9},{9,10},{10,11},{11... | collective-permute-start | bytes 9224 | tf_op jit(solution)/shard_map/ppermute | solution.py:23
  116.8 0.6 collective-permute-done.27
  118.0 1.3 collective-permute-start.32
  119.3 6.4 %collective-permute-start.33 = (f32[1,16,64]{2,1,0:T(8,128)S(1)}, f32[1,16,64]{2,1,0:T(8,128)S(1)}, u32[]{:S(2)}, u32[]{:S(2)}) collective-permute-start(f32[1,16,64]{2,1,0:T(8,128)S(1)} %get-tuple-element.54), channel_id=1, source_target_pairs={{0,8},{8,16},{16,24},{24,32},{32,40},{40,48},{48,56},{56,64},{64,7... | collective-permute-start | bytes 12296 | tf_op jit(solution)/shard_map/ppermute | solution.py:23
  125.7 0.8 collective-permute-done.33
  126.5 1.9 collective-permute-start.34
  128.4 5.0 %collective-permute-start.35 = (f32[4,1,64]{2,1,0:T(1,128)S(1)}, f32[4,1,64]{2,1,0:T(1,128)S(1)}, u32[]{:S(2)}, u32[]{:S(2)}) collective-permute-start(f32[4,1,64]{2,1,0:T(1,128)S(1)} %get-tuple-element.48), channel_id=1, source_target_pairs={{0,1},{1,2},{2,3},{3,4},{4,5},{5,6},{6,7},{8,9},{9,10},{10,11},{11... | collective-permute-start | bytes 3080 | tf_op jit(solution)/shard_map/ppermute | solution.py:23
  134.4 1.3 collective-permute-start.36
  135.7 6.4 %collective-permute-start.37 = (f32[1,16,64]{2,1,0:T(8,128)S(1)}, f32[1,16,64]{2,1,0:T(8,128)S(1)}, u32[]{:S(2)}, u32[]{:S(2)}) collective-permute-start(f32[1,16,64]{2,1,0:T(8,128)S(1)} %get-tuple-element.52), channel_id=1, source_target_pairs={{0,8},{8,16},{16,24},{24,32},{32,40},{40,48},{48,56},{56,64},{64,7... | collective-permute-start | bytes 12296 | tf_op jit(solution)/shard_map/ppermute | solution.py:23
  142.1 46.3 %all-gather.1 = f32[128,1,256]{2,1,0:T(1,128)S(1)} all-gather(f32[1,1,256]{2,1,0:T(1,128)S(1)} %reshape.304), channel_id=1, replica_groups=mesh['xb'=16,'yb'=8] {'xb','yb'}, dimensions={0}, use_global_device_ids=true | all-gather | bytes 132096 | tf_op jit(solution)/shard_map/all_gather | solution.py:122
  188.9 2.1 collective-permute-start.38
  190.9 3.5 %collective-permute-start.39 = (f32[4,1,64]{2,1,0:T(1,128)S(1)}, f32[4,1,64]{2,1,0:T(1,128)S(1)}, u32[]{:S(2)}, u32[]{:S(2)}) collective-permute-start(f32[4,1,64]{2,1,0:T(1,128)S(1)} %get-tuple-element.46), channel_id=1, source_target_pairs={{0,1},{1,2},{2,3},{3,4},{4,5},{5,6},{6,7},{8,9},{9,10},{10,11},{11... | collective-permute-start | bytes 3080 | tf_op jit(solution)/shard_map/ppermute | solution.py:23
  194.5 0.7 collective-permute-done.39
  195.7 34.0 %all-gather = f32[128,1,256]{2,1,0:T(1,128)S(1)} all-gather(f32[1,1,256]{2,1,0:T(1,128)S(1)} %reshape.302), channel_id=1, replica_groups=mesh['xb'=16,'yb'=8] {'xb','yb'}, dimensions={0}, use_global_device_ids=true | all-gather | bytes 132096 | tf_op jit(solution)/shard_map/all_gather | solution.py:121
  230.2 1.0 fusion.147
  231.2 0.7 fusion.23
  231.9 0.7 fusion.39
  232.5 0.7 fusion.55
  233.2 0.7 fusion.71
  233.9 0.7 fusion.87
  234.6 0.7 fusion.103
  235.3 0.7 fusion.119
  236.0 1.6 fusion.213
  239.0 0.6 dynamic-slice_add_fusion
  (110 shorter events, 8.2 us)
Async XLA Ops:
  0.6 20.8 %copy-start = (f32[8,64,256]{2,1,0:T(8,128)S(1)}, f32[8,64,256]{2,1,0:T(8,128)}, u32[]{:S(2)}) copy-start(f32[8,64,256]{2,1,0:T(8,128)} %param.5) | copy-start | bytes 1572868
  1.6 15.2 %collective-permute-start.1 = (f32[1,64,256]{2,1,0:T(8,128)S(1)}, f32[1,64,256]{2,1,0:T(8,128)S(1)}, u32[]{:S(2)}, u32[]{:S(2)}) collective-permute-start(f32[1,64,256]{2,1,0:T(8,128)S(1)} %get-tuple-element.31), channel_id=1, source_target_pairs={{0,8},{8,16},{16,24},{24,32},{32,40},{40,48},{48,56},{56,64},{64,7... | collective-permute-start | bytes 196616 | tf_op jit(solution)/shard_map/ppermute | solution.py:23
  6.0 15.5 %collective-permute-start = (f32[1,64,256]{2,1,0:T(8,128)S(1)}, f32[1,64,256]{2,1,0:T(8,128)S(1)}, u32[]{:S(2)}, u32[]{:S(2)}) collective-permute-start(f32[1,64,256]{2,1,0:T(8,128)S(1)} %get-tuple-element.30), channel_id=1, source_target_pairs={{8,0},{16,8},{24,16},{32,24},{40,32},{48,40},{56,48},{64,56},{72,6... | collective-permute-start | bytes 196616 | tf_op jit(solution)/shard_map/ppermute | solution.py:26
  8.1 17.2 %collective-permute-start.5 = (f32[1,64,256]{2,1,0:T(8,128)S(1)}, f32[1,64,256]{2,1,0:T(8,128)S(1)}, u32[]{:S(2)}, u32[]{:S(2)}) collective-permute-start(f32[1,64,256]{2,1,0:T(8,128)S(1)} %get-tuple-element.33), channel_id=1, source_target_pairs={{0,8},{8,16},{16,24},{24,32},{32,40},{40,48},{48,56},{56,64},{64,7... | collective-permute-start | bytes 196616 | tf_op jit(solution)/shard_map/ppermute | solution.py:23
  12.3 16.1 %collective-permute-start.4 = (f32[1,64,256]{2,1,0:T(8,128)S(1)}, f32[1,64,256]{2,1,0:T(8,128)S(1)}, u32[]{:S(2)}, u32[]{:S(2)}) collective-permute-start(f32[1,64,256]{2,1,0:T(8,128)S(1)} %get-tuple-element.32), channel_id=1, source_target_pairs={{8,0},{16,8},{24,16},{32,24},{40,32},{48,40},{56,48},{64,56},{72,6... | collective-permute-start | bytes 196616 | tf_op jit(solution)/shard_map/ppermute | solution.py:26
  13.7 14.7 %copy-start.3 = (f32[8,64,256]{2,1,0:T(8,128)S(1)}, f32[8,64,256]{2,1,0:T(8,128)}, u32[]{:S(2)}) copy-start(f32[8,64,256]{2,1,0:T(8,128)} %param.3) | copy-start | bytes 1572868
  15.3 43.6 %collective-permute-start.16 = (f32[1,32,128]{2,1,0:T(8,128)S(1)}, f32[1,32,128]{2,1,0:T(8,128)S(1)}, u32[]{:S(2)}, u32[]{:S(2)}) collective-permute-start(f32[1,32,128]{2,1,0:T(8,128)S(1)} %get-tuple-element.45), channel_id=1, source_target_pairs={{8,0},{16,8},{24,16},{32,24},{40,32},{48,40},{56,48},{64,56},{72,6... | collective-permute-start | bytes 49160 | tf_op jit(solution)/shard_map/ppermute | solution.py:26
  16.8 42.1 %collective-permute-start.17 = (f32[1,32,128]{2,1,0:T(8,128)S(1)}, f32[1,32,128]{2,1,0:T(8,128)S(1)}, u32[]{:S(2)}, u32[]{:S(2)}) collective-permute-start(f32[1,32,128]{2,1,0:T(8,128)S(1)} %get-tuple-element.44), channel_id=1, source_target_pairs={{0,8},{8,16},{16,24},{24,32},{32,40},{40,48},{48,56},{56,64},{64,7... | collective-permute-start | bytes 49160 | tf_op jit(solution)/shard_map/ppermute | solution.py:23
  21.5 8.9 %collective-permute-start.2 = (f32[10,1,256]{2,1,0:T(1,128)S(1)}, f32[10,1,256]{2,1,0:T(1,128)S(1)}, u32[]{:S(2)}, u32[]{:S(2)}) collective-permute-start(f32[10,1,256]{2,1,0:T(1,128)S(1)} %get-tuple-element.23), channel_id=1, source_target_pairs={{1,0},{2,1},{3,2},{4,3},{5,4},{6,5},{7,6},{9,8},{10,9},{11,10},{12... | collective-permute-start | bytes 30728 | tf_op jit(solution)/shard_map/ppermute | solution.py:26
  25.4 8.7 %collective-permute-start.3 = (f32[10,1,256]{2,1,0:T(1,128)S(1)}, f32[10,1,256]{2,1,0:T(1,128)S(1)}, u32[]{:S(2)}, u32[]{:S(2)}) collective-permute-start(f32[10,1,256]{2,1,0:T(1,128)S(1)} %get-tuple-element.22), channel_id=1, source_target_pairs={{0,1},{1,2},{2,3},{3,4},{4,5},{5,6},{6,7},{8,9},{9,10},{10,11},{11... | collective-permute-start | bytes 30728 | tf_op jit(solution)/shard_map/ppermute | solution.py:23
  28.5 6.1 %collective-permute-start.6 = (f32[10,1,256]{2,1,0:T(1,128)S(1)}, f32[10,1,256]{2,1,0:T(1,128)S(1)}, u32[]{:S(2)}, u32[]{:S(2)}) collective-permute-start(f32[10,1,256]{2,1,0:T(1,128)S(1)} %get-tuple-element.25), channel_id=1, source_target_pairs={{1,0},{2,1},{3,2},{4,3},{5,4},{6,5},{7,6},{9,8},{10,9},{11,10},{12... | collective-permute-start | bytes 30728 | tf_op jit(solution)/shard_map/ppermute | solution.py:26
  30.4 4.4 %collective-permute-start.7 = (f32[10,1,256]{2,1,0:T(1,128)S(1)}, f32[10,1,256]{2,1,0:T(1,128)S(1)}, u32[]{:S(2)}, u32[]{:S(2)}) collective-permute-start(f32[10,1,256]{2,1,0:T(1,128)S(1)} %get-tuple-element.24), channel_id=1, source_target_pairs={{0,1},{1,2},{2,3},{3,4},{4,5},{5,6},{6,7},{8,9},{9,10},{10,11},{11... | collective-permute-start | bytes 30728 | tf_op jit(solution)/shard_map/ppermute | solution.py:23
  34.6 1.0 copy-start.2
  36.8 5.6 %collective-permute-start.8 = (f32[1,64,256]{2,1,0:T(8,128)S(1)}, f32[1,64,256]{2,1,0:T(8,128)S(1)}, u32[]{:S(2)}, u32[]{:S(2)}) collective-permute-start(f32[1,64,256]{2,1,0:T(8,128)S(1)} %get-tuple-element.29), channel_id=1, source_target_pairs={{8,0},{16,8},{24,16},{32,24},{40,32},{48,40},{56,48},{64,56},{72,6... | collective-permute-start | bytes 196616 | tf_op jit(solution)/shard_map/ppermute | solution.py:26
  38.1 5.6 %collective-permute-start.9 = (f32[1,64,256]{2,1,0:T(8,128)S(1)}, f32[1,64,256]{2,1,0:T(8,128)S(1)}, u32[]{:S(2)}, u32[]{:S(2)}) collective-permute-start(f32[1,64,256]{2,1,0:T(8,128)S(1)} %get-tuple-element.28), channel_id=1, source_target_pairs={{0,8},{8,16},{16,24},{24,32},{32,40},{40,48},{48,56},{56,64},{64,7... | collective-permute-start | bytes 196616 | tf_op jit(solution)/shard_map/ppermute | solution.py:23
  43.7 6.9 %collective-permute-start.10 = (f32[10,1,256]{2,1,0:T(1,128)S(1)}, f32[10,1,256]{2,1,0:T(1,128)S(1)}, u32[]{:S(2)}, u32[]{:S(2)}) collective-permute-start(f32[10,1,256]{2,1,0:T(1,128)S(1)} %get-tuple-element.21), channel_id=1, source_target_pairs={{1,0},{2,1},{3,2},{4,3},{5,4},{6,5},{7,6},{9,8},{10,9},{11,10},{12... | collective-permute-start | bytes 30728 | tf_op jit(solution)/shard_map/ppermute | solution.py:26
  45.7 5.6 %collective-permute-start.11 = (f32[10,1,256]{2,1,0:T(1,128)S(1)}, f32[10,1,256]{2,1,0:T(1,128)S(1)}, u32[]{:S(2)}, u32[]{:S(2)}) collective-permute-start(f32[10,1,256]{2,1,0:T(1,128)S(1)} %get-tuple-element.20), channel_id=1, source_target_pairs={{0,1},{1,2},{2,3},{3,4},{4,5},{5,6},{6,7},{8,9},{9,10},{10,11},{11... | collective-permute-start | bytes 30728 | tf_op jit(solution)/shard_map/ppermute | solution.py:23
  52.9 19.3 %copy-start.1 = (f32[8,64,256]{2,1,0:T(8,128)}, f32[8,64,256]{2,1,0:T(8,128)S(1)}, u32[]{:S(2)}) copy-start(f32[8,64,256]{2,1,0:T(8,128)S(1)} %fusion.181) | copy-start | bytes 1572868
  53.0 12.4 %collective-permute-start.12 = (f32[1,64,256]{2,1,0:T(8,128)S(1)}, f32[1,64,256]{2,1,0:T(8,128)S(1)}, u32[]{:S(2)}, u32[]{:S(2)}) collective-permute-start(f32[1,64,256]{2,1,0:T(8,128)S(1)} %get-tuple-element.27), channel_id=1, source_target_pairs={{8,0},{16,8},{24,16},{32,24},{40,32},{48,40},{56,48},{64,56},{72,6... | collective-permute-start | bytes 196616 | tf_op jit(solution)/shard_map/ppermute | solution.py:26
  54.3 11.1 %collective-permute-start.13 = (f32[1,64,256]{2,1,0:T(8,128)S(1)}, f32[1,64,256]{2,1,0:T(8,128)S(1)}, u32[]{:S(2)}, u32[]{:S(2)}) collective-permute-start(f32[1,64,256]{2,1,0:T(8,128)S(1)} %get-tuple-element.26), channel_id=1, source_target_pairs={{0,8},{8,16},{16,24},{24,32},{32,40},{40,48},{48,56},{56,64},{64,7... | collective-permute-start | bytes 196616 | tf_op jit(solution)/shard_map/ppermute | solution.py:23
  58.9 12.0 %collective-permute-start.18 = (f32[6,1,128]{2,1,0:T(1,128)S(1)}, f32[6,1,128]{2,1,0:T(1,128)S(1)}, u32[]{:S(2)}, u32[]{:S(2)}) collective-permute-start(f32[6,1,128]{2,1,0:T(1,128)S(1)} %get-tuple-element.39), channel_id=1, source_target_pairs={{1,0},{2,1},{3,2},{4,3},{5,4},{6,5},{7,6},{9,8},{10,9},{11,10},{12... | collective-permute-start | bytes 9224 | tf_op jit(solution)/shard_map/ppermute | solution.py:26
  60.9 10.1 %collective-permute-start.19 = (f32[6,1,128]{2,1,0:T(1,128)S(1)}, f32[6,1,128]{2,1,0:T(1,128)S(1)}, u32[]{:S(2)}, u32[]{:S(2)}) collective-permute-start(f32[6,1,128]{2,1,0:T(1,128)S(1)} %get-tuple-element.38), channel_id=1, source_target_pairs={{0,1},{1,2},{2,3},{3,4},{4,5},{5,6},{6,7},{8,9},{9,10},{10,11},{11... | collective-permute-start | bytes 9224 | tf_op jit(solution)/shard_map/ppermute | solution.py:23
  65.4 5.8 %collective-permute-start.14 = (f32[10,1,256]{2,1,0:T(1,128)S(1)}, f32[10,1,256]{2,1,0:T(1,128)S(1)}, u32[]{:S(2)}, u32[]{:S(2)}) collective-permute-start(f32[10,1,256]{2,1,0:T(1,128)S(1)} %get-tuple-element.19), channel_id=1, source_target_pairs={{1,0},{2,1},{3,2},{4,3},{5,4},{6,5},{7,6},{9,8},{10,9},{11,10},{12... | collective-permute-start | bytes 30728 | tf_op jit(solution)/shard_map/ppermute | solution.py:26
  67.3 4.4 %collective-permute-start.15 = (f32[10,1,256]{2,1,0:T(1,128)S(1)}, f32[10,1,256]{2,1,0:T(1,128)S(1)}, u32[]{:S(2)}, u32[]{:S(2)}) collective-permute-start(f32[10,1,256]{2,1,0:T(1,128)S(1)} %get-tuple-element.18), channel_id=1, source_target_pairs={{0,1},{1,2},{2,3},{3,4},{4,5},{5,6},{6,7},{8,9},{9,10},{10,11},{11... | collective-permute-start | bytes 30728 | tf_op jit(solution)/shard_map/ppermute | solution.py:23
  73.9 14.9 %collective-permute-start.20 = (f32[1,32,128]{2,1,0:T(8,128)S(1)}, f32[1,32,128]{2,1,0:T(8,128)S(1)}, u32[]{:S(2)}, u32[]{:S(2)}) collective-permute-start(f32[1,32,128]{2,1,0:T(8,128)S(1)} %get-tuple-element.43), channel_id=1, source_target_pairs={{8,0},{16,8},{24,16},{32,24},{40,32},{48,40},{56,48},{64,56},{72,6... | collective-permute-start | bytes 49160 | tf_op jit(solution)/shard_map/ppermute | solution.py:26
  75.2 13.6 %collective-permute-start.21 = (f32[1,32,128]{2,1,0:T(8,128)S(1)}, f32[1,32,128]{2,1,0:T(8,128)S(1)}, u32[]{:S(2)}, u32[]{:S(2)}) collective-permute-start(f32[1,32,128]{2,1,0:T(8,128)S(1)} %get-tuple-element.42), channel_id=1, source_target_pairs={{0,8},{8,16},{16,24},{24,32},{32,40},{40,48},{48,56},{56,64},{64,7... | collective-permute-start | bytes 49160 | tf_op jit(solution)/shard_map/ppermute | solution.py:23
  81.1 23.5 %collective-permute-start.28 = (f32[1,16,64]{2,1,0:T(8,128)S(1)}, f32[1,16,64]{2,1,0:T(8,128)S(1)}, u32[]{:S(2)}, u32[]{:S(2)}) collective-permute-start(f32[1,16,64]{2,1,0:T(8,128)S(1)} %get-tuple-element.57), channel_id=1, source_target_pairs={{8,0},{16,8},{24,16},{32,24},{40,32},{48,40},{56,48},{64,56},{72,6... | collective-permute-start | bytes 12296 | tf_op jit(solution)/shard_map/ppermute | solution.py:26
  82.4 22.2 %collective-permute-start.29 = (f32[1,16,64]{2,1,0:T(8,128)S(1)}, f32[1,16,64]{2,1,0:T(8,128)S(1)}, u32[]{:S(2)}, u32[]{:S(2)}) collective-permute-start(f32[1,16,64]{2,1,0:T(8,128)S(1)} %get-tuple-element.56), channel_id=1, source_target_pairs={{0,8},{8,16},{16,24},{24,32},{32,40},{40,48},{48,56},{56,64},{64,7... | collective-permute-start | bytes 12296 | tf_op jit(solution)/shard_map/ppermute | solution.py:23
  88.8 6.8 %collective-permute-start.22 = (f32[6,1,128]{2,1,0:T(1,128)S(1)}, f32[6,1,128]{2,1,0:T(1,128)S(1)}, u32[]{:S(2)}, u32[]{:S(2)}) collective-permute-start(f32[6,1,128]{2,1,0:T(1,128)S(1)} %get-tuple-element.37), channel_id=1, source_target_pairs={{1,0},{2,1},{3,2},{4,3},{5,4},{6,5},{7,6},{9,8},{10,9},{11,10},{12... | collective-permute-start | bytes 9224 | tf_op jit(solution)/shard_map/ppermute | solution.py:26
  90.7 5.5 %collective-permute-start.23 = (f32[6,1,128]{2,1,0:T(1,128)S(1)}, f32[6,1,128]{2,1,0:T(1,128)S(1)}, u32[]{:S(2)}, u32[]{:S(2)}) collective-permute-start(f32[6,1,128]{2,1,0:T(1,128)S(1)} %get-tuple-element.36), channel_id=1, source_target_pairs={{0,1},{1,2},{2,3},{3,4},{4,5},{5,6},{6,7},{8,9},{9,10},{10,11},{11... | collective-permute-start | bytes 9224 | tf_op jit(solution)/shard_map/ppermute | solution.py:23
  96.5 92.1 %copy-start.4 = (f32[4,32,128]{2,1,0:T(8,128)}, f32[4,32,128]{2,1,0:T(8,128)S(1)}, u32[]{:S(2)}) copy-start(f32[4,32,128]{2,1,0:T(8,128)S(1)} %fusion.243) | copy-start | bytes 196612
  96.6 14.5 %collective-permute-start.24 = (f32[1,32,128]{2,1,0:T(8,128)S(1)}, f32[1,32,128]{2,1,0:T(8,128)S(1)}, u32[]{:S(2)}, u32[]{:S(2)}) collective-permute-start(f32[1,32,128]{2,1,0:T(8,128)S(1)} %get-tuple-element.41), channel_id=1, source_target_pairs={{8,0},{16,8},{24,16},{32,24},{40,32},{48,40},{56,48},{64,56},{72,6... | collective-permute-start | bytes 49160 | tf_op jit(solution)/shard_map/ppermute | solution.py:26
  97.9 13.2 %collective-permute-start.25 = (f32[1,32,128]{2,1,0:T(8,128)S(1)}, f32[1,32,128]{2,1,0:T(8,128)S(1)}, u32[]{:S(2)}, u32[]{:S(2)}) collective-permute-start(f32[1,32,128]{2,1,0:T(8,128)S(1)} %get-tuple-element.40), channel_id=1, source_target_pairs={{0,8},{8,16},{16,24},{24,32},{32,40},{40,48},{48,56},{56,64},{64,7... | collective-permute-start | bytes 49160 | tf_op jit(solution)/shard_map/ppermute | solution.py:23
  104.6 12.0 %collective-permute-start.30 = (f32[4,1,64]{2,1,0:T(1,128)S(1)}, f32[4,1,64]{2,1,0:T(1,128)S(1)}, u32[]{:S(2)}, u32[]{:S(2)}) collective-permute-start(f32[4,1,64]{2,1,0:T(1,128)S(1)} %get-tuple-element.51), channel_id=1, source_target_pairs={{1,0},{2,1},{3,2},{4,3},{5,4},{6,5},{7,6},{9,8},{10,9},{11,10},{12... | collective-permute-start | bytes 3080 | tf_op jit(solution)/shard_map/ppermute | solution.py:26
  106.6 10.1 %collective-permute-start.31 = (f32[4,1,64]{2,1,0:T(1,128)S(1)}, f32[4,1,64]{2,1,0:T(1,128)S(1)}, u32[]{:S(2)}, u32[]{:S(2)}) collective-permute-start(f32[4,1,64]{2,1,0:T(1,128)S(1)} %get-tuple-element.50), channel_id=1, source_target_pairs={{0,1},{1,2},{2,3},{3,4},{4,5},{5,6},{6,7},{8,9},{9,10},{10,11},{11... | collective-permute-start | bytes 3080 | tf_op jit(solution)/shard_map/ppermute | solution.py:23
  111.1 5.7 %collective-permute-start.26 = (f32[6,1,128]{2,1,0:T(1,128)S(1)}, f32[6,1,128]{2,1,0:T(1,128)S(1)}, u32[]{:S(2)}, u32[]{:S(2)}) collective-permute-start(f32[6,1,128]{2,1,0:T(1,128)S(1)} %get-tuple-element.35), channel_id=1, source_target_pairs={{1,0},{2,1},{3,2},{4,3},{5,4},{6,5},{7,6},{9,8},{10,9},{11,10},{12... | collective-permute-start | bytes 9224 | tf_op jit(solution)/shard_map/ppermute | solution.py:26
  113.0 4.4 %collective-permute-start.27 = (f32[6,1,128]{2,1,0:T(1,128)S(1)}, f32[6,1,128]{2,1,0:T(1,128)S(1)}, u32[]{:S(2)}, u32[]{:S(2)}) collective-permute-start(f32[6,1,128]{2,1,0:T(1,128)S(1)} %get-tuple-element.34), channel_id=1, source_target_pairs={{0,1},{1,2},{2,3},{3,4},{4,5},{5,6},{6,7},{8,9},{9,10},{10,11},{11... | collective-permute-start | bytes 9224 | tf_op jit(solution)/shard_map/ppermute | solution.py:23
  118.0 7.7 %collective-permute-start.32 = (f32[1,16,64]{2,1,0:T(8,128)S(1)}, f32[1,16,64]{2,1,0:T(8,128)S(1)}, u32[]{:S(2)}, u32[]{:S(2)}) collective-permute-start(f32[1,16,64]{2,1,0:T(8,128)S(1)} %get-tuple-element.55), channel_id=1, source_target_pairs={{8,0},{16,8},{24,16},{32,24},{40,32},{48,40},{56,48},{64,56},{72,6... | collective-permute-start | bytes 12296 | tf_op jit(solution)/shard_map/ppermute | solution.py:26
  119.3 7.2 %collective-permute-start.33 = (f32[1,16,64]{2,1,0:T(8,128)S(1)}, f32[1,16,64]{2,1,0:T(8,128)S(1)}, u32[]{:S(2)}, u32[]{:S(2)}) collective-permute-start(f32[1,16,64]{2,1,0:T(8,128)S(1)} %get-tuple-element.54), channel_id=1, source_target_pairs={{0,8},{8,16},{16,24},{24,32},{32,40},{40,48},{48,56},{56,64},{64,7... | collective-permute-start | bytes 12296 | tf_op jit(solution)/shard_map/ppermute | solution.py:23
  126.5 7.2 %collective-permute-start.34 = (f32[4,1,64]{2,1,0:T(1,128)S(1)}, f32[4,1,64]{2,1,0:T(1,128)S(1)}, u32[]{:S(2)}, u32[]{:S(2)}) collective-permute-start(f32[4,1,64]{2,1,0:T(1,128)S(1)} %get-tuple-element.49), channel_id=1, source_target_pairs={{1,0},{2,1},{3,2},{4,3},{5,4},{6,5},{7,6},{9,8},{10,9},{11,10},{12... | collective-permute-start | bytes 3080 | tf_op jit(solution)/shard_map/ppermute | solution.py:26
  128.4 5.8 %collective-permute-start.35 = (f32[4,1,64]{2,1,0:T(1,128)S(1)}, f32[4,1,64]{2,1,0:T(1,128)S(1)}, u32[]{:S(2)}, u32[]{:S(2)}) collective-permute-start(f32[4,1,64]{2,1,0:T(1,128)S(1)} %get-tuple-element.48), channel_id=1, source_target_pairs={{0,1},{1,2},{2,3},{3,4},{4,5},{5,6},{6,7},{8,9},{9,10},{10,11},{11... | collective-permute-start | bytes 3080 | tf_op jit(solution)/shard_map/ppermute | solution.py:23
  134.4 95.8 %copy-start.5 = (f32[2,16,64]{2,1,0:T(8,128)}, f32[2,16,64]{2,1,0:T(8,128)S(1)}, u32[]{:S(2)}) copy-start(f32[2,16,64]{2,1,0:T(8,128)S(1)} %fusion.296) | copy-start | bytes 24580
  134.4 54.4 %collective-permute-start.36 = (f32[1,16,64]{2,1,0:T(8,128)S(1)}, f32[1,16,64]{2,1,0:T(8,128)S(1)}, u32[]{:S(2)}, u32[]{:S(2)}) collective-permute-start(f32[1,16,64]{2,1,0:T(8,128)S(1)} %get-tuple-element.53), channel_id=1, source_target_pairs={{8,0},{16,8},{24,16},{32,24},{40,32},{48,40},{56,48},{64,56},{72,6... | collective-permute-start | bytes 12296 | tf_op jit(solution)/shard_map/ppermute | solution.py:26
  135.7 53.1 %collective-permute-start.37 = (f32[1,16,64]{2,1,0:T(8,128)S(1)}, f32[1,16,64]{2,1,0:T(8,128)S(1)}, u32[]{:S(2)}, u32[]{:S(2)}) collective-permute-start(f32[1,16,64]{2,1,0:T(8,128)S(1)} %get-tuple-element.52), channel_id=1, source_target_pairs={{0,8},{8,16},{16,24},{24,32},{32,40},{40,48},{48,56},{56,64},{64,7... | collective-permute-start | bytes 12296 | tf_op jit(solution)/shard_map/ppermute | solution.py:23
  188.9 5.6 %collective-permute-start.38 = (f32[4,1,64]{2,1,0:T(1,128)S(1)}, f32[4,1,64]{2,1,0:T(1,128)S(1)}, u32[]{:S(2)}, u32[]{:S(2)}) collective-permute-start(f32[4,1,64]{2,1,0:T(1,128)S(1)} %get-tuple-element.47), channel_id=1, source_target_pairs={{1,0},{2,1},{3,2},{4,3},{5,4},{6,5},{7,6},{9,8},{10,9},{11,10},{12... | collective-permute-start | bytes 3080 | tf_op jit(solution)/shard_map/ppermute | solution.py:26
  190.9 4.2 %collective-permute-start.39 = (f32[4,1,64]{2,1,0:T(1,128)S(1)}, f32[4,1,64]{2,1,0:T(1,128)S(1)}, u32[]{:S(2)}, u32[]{:S(2)}) collective-permute-start(f32[4,1,64]{2,1,0:T(1,128)S(1)} %get-tuple-element.46), channel_id=1, source_target_pairs={{0,1},{1,2},{2,3},{3,4},{4,5},{5,6},{6,7},{8,9},{9,10},{10,11},{11... | collective-permute-start | bytes 3080 | tf_op jit(solution)/shard_map/ppermute | solution.py:23
where the time goes:
time: 241 us; the launch traced here: 240 us
  starting transfers between devices  129 us (54%)
  blocking collectives  80.2 us (33%)
  other arithmetic  15.3 us (6%)
  waiting for transfers between devices  6.04 us (3%)
  matrix products  3.23 us (1%)
  between operations  3.06 us (1%)
  local copies, waits for them, and re-layouts  2.89 us (1%)
    ppermute x20, starting transfers between devices, with_halo(): lax.ppermute(lax.slice_in_dim(block, block.shape[dim] - width, None, axis...  94.7 us
    all_gather x1, blocking collectives, collect_grid(): lax.all_gather(coefficient.reshape(1, -1), ('xb', 'yb'), axis=0, tiled=True)  46.3 us
    ppermute x20, starting transfers between devices, with_halo(): lax.ppermute(lax.slice_in_dim(block, 0, width, axis=dim), axis, backward)  34.1 us
    all_gather x1, blocking collectives, collect_grid(): lax.all_gather(right_side.reshape(1, -1), ('xb', 'yb'), axis=0, tiled=True)  34 us
    ppermute x20, waiting for transfers between devices, with_halo(): lax.ppermute(lax.slice_in_dim(block, block.shape[dim] - width, None, axis...  5.99 us
  transfers between devices with their start and end apart: 40, of which 9 were waited for; matrix products, arithmetic and copies ran while one was open for 3% of the time, Pallas kernels for 0%

commit v1 on v0

--- a/solution.py
+++ b/solution.py
@@ -119,7 +119,15 @@
     count_y = lax.axis_size("yb")
     flat = (
         lax.all_gather(right_side.reshape(1, -1), ("xb", "yb"), axis=0, tiled=True),
-        lax.all_gather(coefficient.reshape(1, -1), ("xb", "yb"), axis=0, tiled=True),
+        jnp.concatenate(
+            lax.all_to_all(
+                jnp.stack([coefficient.reshape(1, -1)] * lax.axis_size(("xb", "yb"))),
+                ("xb", "yb"),
+                0,
+                0,
+            ),
+            axis=0,
+        ),
     )
     return tuple(
         (

time: 241 us -> 220 us (0.913)
  blocking collectives: 80.2 us -> 42.8 us
  starting transfers between devices: 129 us -> 145 us
    all_gather x1 -> x0, blocking collectives: 46.3 us -> none  [collect_grid(): lax.all_gather(coefficient.reshape(1, -1), ('xb', 'yb'), axis=0, tiled=True)]
    all_to_all x0 -> x1, starting transfers between devices: none -> 17.4 us  [collect_grid(): lax.all_to_all(jnp.stack([coefficient.reshape(1, -1)] * lax.axis_size(('x...]
    all_gather x1, blocking collectives: 34 us -> 42.8 us  [collect_grid(): lax.all_gather(right_side.reshape(1, -1), ('xb', 'yb'), axis=0, tiled=True)]
    ppermute x20, starting transfers between devices: 94.7 us -> 91.4 us  [with_halo(): lax.ppermute(lax.slice_in_dim(block, block.shape[dim] - width, None, axis...]
  transfers between devices with their start and end apart: 40 -> 41, of which waited for: 9 -> 9; matrix products, arithmetic and copies ran while one was open for 3% -> 4% of each run, Pallas kernels for 0% -> 0%
where the time goes in v1:
time: 220 us; the launch traced here: 219 us
  starting transfers between devices  145 us (66%)
  blocking collectives  42.8 us (19%)
  other arithmetic  15.3 us (7%)
  waiting for transfers between devices  5.8 us (3%)
  local copies, waits for them, and re-layouts  3.63 us (2%)
  matrix products  3.23 us (1%)
  between operations  2.96 us (1%)
    ppermute x20, starting transfers between devices, with_halo(): lax.ppermute(lax.slice_in_dim(block, block.shape[dim] - width, None, axis...  91.4 us
    all_gather x1, blocking collectives, collect_grid(): lax.all_gather(right_side.reshape(1, -1), ('xb', 'yb'), axis=0, tiled=True)  42.8 us
    ppermute x20, starting transfers between devices, with_halo(): lax.ppermute(lax.slice_in_dim(block, 0, width, axis=dim), axis, backward)  36.1 us
    all_to_all x1, starting transfers between devices, collect_grid(): lax.all_to_all(jnp.stack([coefficient.reshape(1, -1)] * lax.axis_size(('x...  17.4 us
    ppermute x20, waiting for transfers between devices, with_halo(): lax.ppermute(lax.slice_in_dim(block, block.shape[dim] - width, None, axis...  5.75 us
    add x7, other arithmetic, coarse_solve(): field + jacobi_weight * (right_side - apply_operator(extend(field), field...  4.78 us
  transfers between devices with their start and end apart: 41, of which 9 were waited for; matrix products, arithmetic and copies ran while one was open for 4% of the time, Pallas kernels for 0%

profile of v1, /device:TPU:1, one launch (start us, length us, event | category | flops | bytes accessed | tf_op | source)
XLA Modules:
  0.0 218.6 jit_solution(17982482382873073655)
XLA Ops:
  0.6 0.9 fusion.348
  1.6 4.4 %collective-permute-start.1 = (f32[1,64,256]{2,1,0:T(8,128)S(1)}, f32[1,64,256]{2,1,0:T(8,128)S(1)}, u32[]{:S(2)}, u32[]{:S(2)}) collective-permute-start(f32[1,64,256]{2,1,0:T(8,128)S(1)} %get-tuple-element.31), channel_id=1, source_target_pairs={{0,8},{8,16},{16,24},{24,32},{32,40},{40,48},{48,56},{56,64},{64,7... | collective-permute-start | bytes 196616 | tf_op jit(solution)/shard_map/ppermute | solution.py:23
  6.0 1.3 collective-permute-start
  7.3 0.9 fusion.349
  8.1 4.2 %collective-permute-start.5 = (f32[1,64,256]{2,1,0:T(8,128)S(1)}, f32[1,64,256]{2,1,0:T(8,128)S(1)}, u32[]{:S(2)}, u32[]{:S(2)}) collective-permute-start(f32[1,64,256]{2,1,0:T(8,128)S(1)} %get-tuple-element.33), channel_id=1, source_target_pairs={{0,8},{8,16},{16,24},{24,32},{32,40},{40,48},{48,56},{56,64},{64,7... | collective-permute-start | bytes 196616 | tf_op jit(solution)/shard_map/ppermute | solution.py:23
  12.3 1.3 collective-permute-start.4
  13.7 1.4 fusion.217
  15.3 1.3 collective-permute-start.16
  16.8 4.6 %collective-permute-start.17 = (f32[1,32,128]{2,1,0:T(8,128)S(1)}, f32[1,32,128]{2,1,0:T(8,128)S(1)}, u32[]{:S(2)}, u32[]{:S(2)}) collective-permute-start(f32[1,32,128]{2,1,0:T(8,128)S(1)} %get-tuple-element.44), channel_id=1, source_target_pairs={{0,8},{8,16},{16,24},{24,32},{32,40},{40,48},{48,56},{56,64},{64,7... | collective-permute-start | bytes 49160 | tf_op jit(solution)/shard_map/ppermute | solution.py:23
  21.5 3.8 %collective-permute-start.2 = (f32[10,1,256]{2,1,0:T(1,128)S(1)}, f32[10,1,256]{2,1,0:T(1,128)S(1)}, u32[]{:S(2)}, u32[]{:S(2)}) collective-permute-start(f32[10,1,256]{2,1,0:T(1,128)S(1)} %get-tuple-element.23), channel_id=1, source_target_pairs={{1,0},{2,1},{3,2},{4,3},{5,4},{6,5},{7,6},{9,8},{10,9},{11,10},{12... | collective-permute-start | bytes 30728 | tf_op jit(solution)/shard_map/ppermute | solution.py:26
  25.4 3.0 %collective-permute-start.3 = (f32[10,1,256]{2,1,0:T(1,128)S(1)}, f32[10,1,256]{2,1,0:T(1,128)S(1)}, u32[]{:S(2)}, u32[]{:S(2)}) collective-permute-start(f32[10,1,256]{2,1,0:T(1,128)S(1)} %get-tuple-element.22), channel_id=1, source_target_pairs={{0,1},{1,2},{2,3},{3,4},{4,5},{5,6},{6,7},{8,9},{9,10},{10,11},{11... | collective-permute-start | bytes 30728 | tf_op jit(solution)/shard_map/ppermute | solution.py:23
  28.5 1.9 collective-permute-start.6
  30.4 3.6 %collective-permute-start.7 = (f32[10,1,256]{2,1,0:T(1,128)S(1)}, f32[10,1,256]{2,1,0:T(1,128)S(1)}, u32[]{:S(2)}, u32[]{:S(2)}) collective-permute-start(f32[10,1,256]{2,1,0:T(1,128)S(1)} %get-tuple-element.24), channel_id=1, source_target_pairs={{0,1},{1,2},{2,3},{3,4},{4,5},{5,6},{6,7},{8,9},{9,10},{10,11},{11... | collective-permute-start | bytes 30728 | tf_op jit(solution)/shard_map/ppermute | solution.py:23
  35.6 1.2 fusion.342
  36.8 1.3 collective-permute-start.8
  38.1 4.3 %collective-permute-start.9 = (f32[1,64,256]{2,1,0:T(8,128)S(1)}, f32[1,64,256]{2,1,0:T(8,128)S(1)}, u32[]{:S(2)}, u32[]{:S(2)}) collective-permute-start(f32[1,64,256]{2,1,0:T(8,128)S(1)} %get-tuple-element.28), channel_id=1, source_target_pairs={{0,8},{8,16},{16,24},{24,32},{32,40},{40,48},{48,56},{56,64},{64,7... | collective-permute-start | bytes 196616 | tf_op jit(solution)/shard_map/ppermute | solution.py:23
  42.4 1.3 collective-permute-done.9
  43.7 1.9 collective-permute-start.10
  45.7 4.8 %collective-permute-start.11 = (f32[10,1,256]{2,1,0:T(1,128)S(1)}, f32[10,1,256]{2,1,0:T(1,128)S(1)}, u32[]{:S(2)}, u32[]{:S(2)}) collective-permute-start(f32[10,1,256]{2,1,0:T(1,128)S(1)} %get-tuple-element.20), channel_id=1, source_target_pairs={{0,1},{1,2},{2,3},{3,4},{4,5},{5,6},{6,7},{8,9},{9,10},{10,11},{11... | collective-permute-start | bytes 30728 | tf_op jit(solution)/shard_map/ppermute | solution.py:23
  50.6 0.6 collective-permute-done.11
  51.7 1.2 fusion.181
  53.0 1.3 collective-permute-start.12
  54.3 4.6 %collective-permute-start.13 = (f32[1,64,256]{2,1,0:T(8,128)S(1)}, f32[1,64,256]{2,1,0:T(8,128)S(1)}, u32[]{:S(2)}, u32[]{:S(2)}) collective-permute-start(f32[1,64,256]{2,1,0:T(8,128)S(1)} %get-tuple-element.26), channel_id=1, source_target_pairs={{0,8},{8,16},{16,24},{24,32},{32,40},{40,48},{48,56},{56,64},{64,7... | collective-permute-start | bytes 196616 | tf_op jit(solution)/shard_map/ppermute | solution.py:23
  58.9 1.9 collective-permute-start.18
  60.9 4.5 %collective-permute-start.19 = (f32[6,1,128]{2,1,0:T(1,128)S(1)}, f32[6,1,128]{2,1,0:T(1,128)S(1)}, u32[]{:S(2)}, u32[]{:S(2)}) collective-permute-start(f32[6,1,128]{2,1,0:T(1,128)S(1)} %get-tuple-element.38), channel_id=1, source_target_pairs={{0,1},{1,2},{2,3},{3,4},{4,5},{5,6},{6,7},{8,9},{9,10},{10,11},{11... | collective-permute-start | bytes 9224 | tf_op jit(solution)/shard_map/ppermute | solution.py:23
  65.4 1.9 collective-permute-start.14
  67.3 3.6 %collective-permute-start.15 = (f32[10,1,256]{2,1,0:T(1,128)S(1)}, f32[10,1,256]{2,1,0:T(1,128)S(1)}, u32[]{:S(2)}, u32[]{:S(2)}) collective-permute-start(f32[10,1,256]{2,1,0:T(1,128)S(1)} %get-tuple-element.18), channel_id=1, source_target_pairs={{0,1},{1,2},{2,3},{3,4},{4,5},{5,6},{6,7},{8,9},{9,10},{10,11},{11... | collective-permute-start | bytes 30728 | tf_op jit(solution)/shard_map/ppermute | solution.py:23
  72.2 1.1 fusion.166
  73.9 1.3 collective-permute-start.20
  75.2 5.8 %collective-permute-start.21 = (f32[1,32,128]{2,1,0:T(8,128)S(1)}, f32[1,32,128]{2,1,0:T(8,128)S(1)}, u32[]{:S(2)}, u32[]{:S(2)}) collective-permute-start(f32[1,32,128]{2,1,0:T(8,128)S(1)} %get-tuple-element.42), channel_id=1, source_target_pairs={{0,8},{8,16},{16,24},{24,32},{32,40},{40,48},{48,56},{56,64},{64,7... | collective-permute-start | bytes 49160 | tf_op jit(solution)/shard_map/ppermute | solution.py:23
  81.1 1.3 collective-permute-start.28
  82.4 6.4 %collective-permute-start.29 = (f32[1,16,64]{2,1,0:T(8,128)S(1)}, f32[1,16,64]{2,1,0:T(8,128)S(1)}, u32[]{:S(2)}, u32[]{:S(2)}) collective-permute-start(f32[1,16,64]{2,1,0:T(8,128)S(1)} %get-tuple-element.56), channel_id=1, source_target_pairs={{0,8},{8,16},{16,24},{24,32},{32,40},{40,48},{48,56},{56,64},{64,7... | collective-permute-start | bytes 12296 | tf_op jit(solution)/shard_map/ppermute | solution.py:23
  88.8 1.9 collective-permute-start.22
  90.7 4.8 %collective-permute-start.23 = (f32[6,1,128]{2,1,0:T(1,128)S(1)}, f32[6,1,128]{2,1,0:T(1,128)S(1)}, u32[]{:S(2)}, u32[]{:S(2)}) collective-permute-start(f32[6,1,128]{2,1,0:T(1,128)S(1)} %get-tuple-element.36), channel_id=1, source_target_pairs={{0,1},{1,2},{2,3},{3,4},{4,5},{5,6},{6,7},{8,9},{9,10},{10,11},{11... | collective-permute-start | bytes 9224 | tf_op jit(solution)/shard_map/ppermute | solution.py:23
  95.6 0.6 collective-permute-done.23
  96.6 1.3 collective-permute-start.24
  97.9 6.7 %collective-permute-start.25 = (f32[1,32,128]{2,1,0:T(8,128)S(1)}, f32[1,32,128]{2,1,0:T(8,128)S(1)}, u32[]{:S(2)}, u32[]{:S(2)}) collective-permute-start(f32[1,32,128]{2,1,0:T(8,128)S(1)} %get-tuple-element.40), channel_id=1, source_target_pairs={{0,8},{8,16},{16,24},{24,32},{32,40},{40,48},{48,56},{56,64},{64,7... | collective-permute-start | bytes 49160 | tf_op jit(solution)/shard_map/ppermute | solution.py:23
  104.6 1.9 collective-permute-start.30
  106.6 4.5 %collective-permute-start.31 = (f32[4,1,64]{2,1,0:T(1,128)S(1)}, f32[4,1,64]{2,1,0:T(1,128)S(1)}, u32[]{:S(2)}, u32[]{:S(2)}) collective-permute-start(f32[4,1,64]{2,1,0:T(1,128)S(1)} %get-tuple-element.50), channel_id=1, source_target_pairs={{0,1},{1,2},{2,3},{3,4},{4,5},{5,6},{6,7},{8,9},{9,10},{10,11},{11... | collective-permute-start | bytes 3080 | tf_op jit(solution)/shard_map/ppermute | solution.py:23
  111.1 1.9 collective-permute-start.26
  113.0 3.6 %collective-permute-start.27 = (f32[6,1,128]{2,1,0:T(1,128)S(1)}, f32[6,1,128]{2,1,0:T(1,128)S(1)}, u32[]{:S(2)}, u32[]{:S(2)}) collective-permute-start(f32[6,1,128]{2,1,0:T(1,128)S(1)} %get-tuple-element.34), channel_id=1, source_target_pairs={{0,1},{1,2},{2,3},{3,4},{4,5},{5,6},{6,7},{8,9},{9,10},{10,11},{11... | collective-permute-start | bytes 9224 | tf_op jit(solution)/shard_map/ppermute | solution.py:23
  118.0 1.3 collective-permute-start.32
  119.3 6.4 %collective-permute-start.33 = (f32[1,16,64]{2,1,0:T(8,128)S(1)}, f32[1,16,64]{2,1,0:T(8,128)S(1)}, u32[]{:S(2)}, u32[]{:S(2)}) collective-permute-start(f32[1,16,64]{2,1,0:T(8,128)S(1)} %get-tuple-element.54), channel_id=1, source_target_pairs={{0,8},{8,16},{16,24},{24,32},{32,40},{40,48},{48,56},{56,64},{64,7... | collective-permute-start | bytes 12296 | tf_op jit(solution)/shard_map/ppermute | solution.py:23
  125.7 0.8 collective-permute-done.33
  126.5 1.9 collective-permute-start.34
  128.4 5.0 %collective-permute-start.35 = (f32[4,1,64]{2,1,0:T(1,128)S(1)}, f32[4,1,64]{2,1,0:T(1,128)S(1)}, u32[]{:S(2)}, u32[]{:S(2)}) collective-permute-start(f32[4,1,64]{2,1,0:T(1,128)S(1)} %get-tuple-element.48), channel_id=1, source_target_pairs={{0,1},{1,2},{2,3},{3,4},{4,5},{5,6},{6,7},{8,9},{9,10},{10,11},{11... | collective-permute-start | bytes 3080 | tf_op jit(solution)/shard_map/ppermute | solution.py:23
  133.7 0.7 stack.3
  134.4 17.4 %all-to-all-start = ((f32[128,1,256]{2,1,0:T(1,128)}), f32[128,1,256]{2,1,0:T(1,128)S(1)}, u32[]{:S(2)}, u32[]{:S(2)}) async-start(f32[128,1,256]{2,1,0:T(1,128)} %stack.3), calls=%async_computation | async-start | bytes 262144 | tf_op jit(solution)/shard_map/all_to_all | solution.py:123
  152.1 1.3 collective-permute-start.36
  153.4 4.0 %collective-permute-start.37 = (f32[1,16,64]{2,1,0:T(8,128)S(1)}, f32[1,16,64]{2,1,0:T(8,128)S(1)}, u32[]{:S(2)}, u32[]{:S(2)}) collective-permute-start(f32[1,16,64]{2,1,0:T(8,128)S(1)} %get-tuple-element.52), channel_id=1, source_target_pairs={{0,8},{8,16},{16,24},{24,32},{32,40},{40,48},{48,56},{56,64},{64,7... | collective-permute-start | bytes 12296 | tf_op jit(solution)/shard_map/ppermute | solution.py:23
  157.4 0.8 collective-permute-done.37
  158.2 4.1 %collective-permute-start.38 = (f32[4,1,64]{2,1,0:T(1,128)S(1)}, f32[4,1,64]{2,1,0:T(1,128)S(1)}, u32[]{:S(2)}, u32[]{:S(2)}) collective-permute-start(f32[4,1,64]{2,1,0:T(1,128)S(1)} %get-tuple-element.47), channel_id=1, source_target_pairs={{1,0},{2,1},{3,2},{4,3},{5,4},{6,5},{7,6},{9,8},{10,9},{11,10},{12... | collective-permute-start | bytes 3080 | tf_op jit(solution)/shard_map/ppermute | solution.py:26
  162.3 2.5 %collective-permute-start.39 = (f32[4,1,64]{2,1,0:T(1,128)S(1)}, f32[4,1,64]{2,1,0:T(1,128)S(1)}, u32[]{:S(2)}, u32[]{:S(2)}) collective-permute-start(f32[4,1,64]{2,1,0:T(1,128)S(1)} %get-tuple-element.46), channel_id=1, source_target_pairs={{0,1},{1,2},{2,3},{3,4},{4,5},{5,6},{6,7},{8,9},{9,10},{10,11},{11... | collective-permute-start | bytes 3080 | tf_op jit(solution)/shard_map/ppermute | solution.py:23
  166.0 42.8 %all-gather = f32[128,1,256]{2,1,0:T(1,128)S(1)} all-gather(f32[1,1,256]{2,1,0:T(1,128)S(1)} %reshape.302), channel_id=1, replica_groups=mesh['xb'=16,'yb'=8] {'xb','yb'}, dimensions={0}, use_global_device_ids=true | all-gather | bytes 132096 | tf_op jit(solution)/shard_map/all_gather | solution.py:121
  209.4 1.0 fusion.147
  210.4 0.7 fusion.23
  211.0 0.7 fusion.39
  211.7 0.7 fusion.55
  212.4 0.7 fusion.71
  213.1 0.7 fusion.87
  213.8 0.7 fusion.103
  214.5 0.7 fusion.119
  215.2 1.6 fusion.213
  218.0 0.6 dynamic-slice_add_fusion
  (112 shorter events, 8.5 us)
Async XLA Ops:
  0.6 20.8 %copy-start = (f32[8,64,256]{2,1,0:T(8,128)S(1)}, f32[8,64,256]{2,1,0:T(8,128)}, u32[]{:S(2)}) copy-start(f32[8,64,256]{2,1,0:T(8,128)} %param.5) | copy-start | bytes 1572868
  1.6 15.2 %collective-permute-start.1 = (f32[1,64,256]{2,1,0:T(8,128)S(1)}, f32[1,64,256]{2,1,0:T(8,128)S(1)}, u32[]{:S(2)}, u32[]{:S(2)}) collective-permute-start(f32[1,64,256]{2,1,0:T(8,128)S(1)} %get-tuple-element.31), channel_id=1, source_target_pairs={{0,8},{8,16},{16,24},{24,32},{32,40},{40,48},{48,56},{56,64},{64,7... | collective-permute-start | bytes 196616 | tf_op jit(solution)/shard_map/ppermute | solution.py:23
  6.0 15.5 %collective-permute-start = (f32[1,64,256]{2,1,0:T(8,128)S(1)}, f32[1,64,256]{2,1,0:T(8,128)S(1)}, u32[]{:S(2)}, u32[]{:S(2)}) collective-permute-start(f32[1,64,256]{2,1,0:T(8,128)S(1)} %get-tuple-element.30), channel_id=1, source_target_pairs={{8,0},{16,8},{24,16},{32,24},{40,32},{48,40},{56,48},{64,56},{72,6... | collective-permute-start | bytes 196616 | tf_op jit(solution)/shard_map/ppermute | solution.py:26
  8.1 17.2 %collective-permute-start.5 = (f32[1,64,256]{2,1,0:T(8,128)S(1)}, f32[1,64,256]{2,1,0:T(8,128)S(1)}, u32[]{:S(2)}, u32[]{:S(2)}) collective-permute-start(f32[1,64,256]{2,1,0:T(8,128)S(1)} %get-tuple-element.33), channel_id=1, source_target_pairs={{0,8},{8,16},{16,24},{24,32},{32,40},{40,48},{48,56},{56,64},{64,7... | collective-permute-start | bytes 196616 | tf_op jit(solution)/shard_map/ppermute | solution.py:23
  12.3 16.1 %collective-permute-start.4 = (f32[1,64,256]{2,1,0:T(8,128)S(1)}, f32[1,64,256]{2,1,0:T(8,128)S(1)}, u32[]{:S(2)}, u32[]{:S(2)}) collective-permute-start(f32[1,64,256]{2,1,0:T(8,128)S(1)} %get-tuple-element.32), channel_id=1, source_target_pairs={{8,0},{16,8},{24,16},{32,24},{40,32},{48,40},{56,48},{64,56},{72,6... | collective-permute-start | bytes 196616 | tf_op jit(solution)/shard_map/ppermute | solution.py:26
  13.7 14.7 %copy-start.3 = (f32[8,64,256]{2,1,0:T(8,128)S(1)}, f32[8,64,256]{2,1,0:T(8,128)}, u32[]{:S(2)}) copy-start(f32[8,64,256]{2,1,0:T(8,128)} %param.3) | copy-start | bytes 1572868
  15.3 43.6 %collective-permute-start.16 = (f32[1,32,128]{2,1,0:T(8,128)S(1)}, f32[1,32,128]{2,1,0:T(8,128)S(1)}, u32[]{:S(2)}, u32[]{:S(2)}) collective-permute-start(f32[1,32,128]{2,1,0:T(8,128)S(1)} %get-tuple-element.45), channel_id=1, source_target_pairs={{8,0},{16,8},{24,16},{32,24},{40,32},{48,40},{56,48},{64,56},{72,6... | collective-permute-start | bytes 49160 | tf_op jit(solution)/shard_map/ppermute | solution.py:26
  16.8 42.1 %collective-permute-start.17 = (f32[1,32,128]{2,1,0:T(8,128)S(1)}, f32[1,32,128]{2,1,0:T(8,128)S(1)}, u32[]{:S(2)}, u32[]{:S(2)}) collective-permute-start(f32[1,32,128]{2,1,0:T(8,128)S(1)} %get-tuple-element.44), channel_id=1, source_target_pairs={{0,8},{8,16},{16,24},{24,32},{32,40},{40,48},{48,56},{56,64},{64,7... | collective-permute-start | bytes 49160 | tf_op jit(solution)/shard_map/ppermute | solution.py:23
  21.5 8.9 %collective-permute-start.2 = (f32[10,1,256]{2,1,0:T(1,128)S(1)}, f32[10,1,256]{2,1,0:T(1,128)S(1)}, u32[]{:S(2)}, u32[]{:S(2)}) collective-permute-start(f32[10,1,256]{2,1,0:T(1,128)S(1)} %get-tuple-element.23), channel_id=1, source_target_pairs={{1,0},{2,1},{3,2},{4,3},{5,4},{6,5},{7,6},{9,8},{10,9},{11,10},{12... | collective-permute-start | bytes 30728 | tf_op jit(solution)/shard_map/ppermute | solution.py:26
  25.4 8.7 %collective-permute-start.3 = (f32[10,1,256]{2,1,0:T(1,128)S(1)}, f32[10,1,256]{2,1,0:T(1,128)S(1)}, u32[]{:S(2)}, u32[]{:S(2)}) collective-permute-start(f32[10,1,256]{2,1,0:T(1,128)S(1)} %get-tuple-element.22), channel_id=1, source_target_pairs={{0,1},{1,2},{2,3},{3,4},{4,5},{5,6},{6,7},{8,9},{9,10},{10,11},{11... | collective-permute-start | bytes 30728 | tf_op jit(solution)/shard_map/ppermute | solution.py:23
  28.5 6.1 %collective-permute-start.6 = (f32[10,1,256]{2,1,0:T(1,128)S(1)}, f32[10,1,256]{2,1,0:T(1,128)S(1)}, u32[]{:S(2)}, u32[]{:S(2)}) collective-permute-start(f32[10,1,256]{2,1,0:T(1,128)S(1)} %get-tuple-element.25), channel_id=1, source_target_pairs={{1,0},{2,1},{3,2},{4,3},{5,4},{6,5},{7,6},{9,8},{10,9},{11,10},{12... | collective-permute-start | bytes 30728 | tf_op jit(solution)/shard_map/ppermute | solution.py:26
  30.4 4.4 %collective-permute-start.7 = (f32[10,1,256]{2,1,0:T(1,128)S(1)}, f32[10,1,256]{2,1,0:T(1,128)S(1)}, u32[]{:S(2)}, u32[]{:S(2)}) collective-permute-start(f32[10,1,256]{2,1,0:T(1,128)S(1)} %get-tuple-element.24), channel_id=1, source_target_pairs={{0,1},{1,2},{2,3},{3,4},{4,5},{5,6},{6,7},{8,9},{9,10},{10,11},{11... | collective-permute-start | bytes 30728 | tf_op jit(solution)/shard_map/ppermute | solution.py:23
  34.6 1.0 copy-start.2
  36.8 5.6 %collective-permute-start.8 = (f32[1,64,256]{2,1,0:T(8,128)S(1)}, f32[1,64,256]{2,1,0:T(8,128)S(1)}, u32[]{:S(2)}, u32[]{:S(2)}) collective-permute-start(f32[1,64,256]{2,1,0:T(8,128)S(1)} %get-tuple-element.29), channel_id=1, source_target_pairs={{8,0},{16,8},{24,16},{32,24},{40,32},{48,40},{56,48},{64,56},{72,6... | collective-permute-start | bytes 196616 | tf_op jit(solution)/shard_map/ppermute | solution.py:26
  38.1 5.6 %collective-permute-start.9 = (f32[1,64,256]{2,1,0:T(8,128)S(1)}, f32[1,64,256]{2,1,0:T(8,128)S(1)}, u32[]{:S(2)}, u32[]{:S(2)}) collective-permute-start(f32[1,64,256]{2,1,0:T(8,128)S(1)} %get-tuple-element.28), channel_id=1, source_target_pairs={{0,8},{8,16},{16,24},{24,32},{32,40},{40,48},{48,56},{56,64},{64,7... | collective-permute-start | bytes 196616 | tf_op jit(solution)/shard_map/ppermute | solution.py:23
  43.7 6.9 %collective-permute-start.10 = (f32[10,1,256]{2,1,0:T(1,128)S(1)}, f32[10,1,256]{2,1,0:T(1,128)S(1)}, u32[]{:S(2)}, u32[]{:S(2)}) collective-permute-start(f32[10,1,256]{2,1,0:T(1,128)S(1)} %get-tuple-element.21), channel_id=1, source_target_pairs={{1,0},{2,1},{3,2},{4,3},{5,4},{6,5},{7,6},{9,8},{10,9},{11,10},{12... | collective-permute-start | bytes 30728 | tf_op jit(solution)/shard_map/ppermute | solution.py:26
  45.7 5.6 %collective-permute-start.11 = (f32[10,1,256]{2,1,0:T(1,128)S(1)}, f32[10,1,256]{2,1,0:T(1,128)S(1)}, u32[]{:S(2)}, u32[]{:S(2)}) collective-permute-start(f32[10,1,256]{2,1,0:T(1,128)S(1)} %get-tuple-element.20), channel_id=1, source_target_pairs={{0,1},{1,2},{2,3},{3,4},{4,5},{5,6},{6,7},{8,9},{9,10},{10,11},{11... | collective-permute-start | bytes 30728 | tf_op jit(solution)/shard_map/ppermute | solution.py:23
  52.9 19.3 %copy-start.1 = (f32[8,64,256]{2,1,0:T(8,128)}, f32[8,64,256]{2,1,0:T(8,128)S(1)}, u32[]{:S(2)}) copy-start(f32[8,64,256]{2,1,0:T(8,128)S(1)} %fusion.181) | copy-start | bytes 1572868
  53.0 12.4 %collective-permute-start.12 = (f32[1,64,256]{2,1,0:T(8,128)S(1)}, f32[1,64,256]{2,1,0:T(8,128)S(1)}, u32[]{:S(2)}, u32[]{:S(2)}) collective-permute-start(f32[1,64,256]{2,1,0:T(8,128)S(1)} %get-tuple-element.27), channel_id=1, source_target_pairs={{8,0},{16,8},{24,16},{32,24},{40,32},{48,40},{56,48},{64,56},{72,6... | collective-permute-start | bytes 196616 | tf_op jit(solution)/shard_map/ppermute | solution.py:26
  54.3 11.1 %collective-permute-start.13 = (f32[1,64,256]{2,1,0:T(8,128)S(1)}, f32[1,64,256]{2,1,0:T(8,128)S(1)}, u32[]{:S(2)}, u32[]{:S(2)}) collective-permute-start(f32[1,64,256]{2,1,0:T(8,128)S(1)} %get-tuple-element.26), channel_id=1, source_target_pairs={{0,8},{8,16},{16,24},{24,32},{32,40},{40,48},{48,56},{56,64},{64,7... | collective-permute-start | bytes 196616 | tf_op jit(solution)/shard_map/ppermute | solution.py:23
  58.9 12.0 %collective-permute-start.18 = (f32[6,1,128]{2,1,0:T(1,128)S(1)}, f32[6,1,128]{2,1,0:T(1,128)S(1)}, u32[]{:S(2)}, u32[]{:S(2)}) collective-permute-start(f32[6,1,128]{2,1,0:T(1,128)S(1)} %get-tuple-element.39), channel_id=1, source_target_pairs={{1,0},{2,1},{3,2},{4,3},{5,4},{6,5},{7,6},{9,8},{10,9},{11,10},{12... | collective-permute-start | bytes 9224 | tf_op jit(solution)/shard_map/ppermute | solution.py:26
  60.9 10.1 %collective-permute-start.19 = (f32[6,1,128]{2,1,0:T(1,128)S(1)}, f32[6,1,128]{2,1,0:T(1,128)S(1)}, u32[]{:S(2)}, u32[]{:S(2)}) collective-permute-start(f32[6,1,128]{2,1,0:T(1,128)S(1)} %get-tuple-element.38), channel_id=1, source_target_pairs={{0,1},{1,2},{2,3},{3,4},{4,5},{5,6},{6,7},{8,9},{9,10},{10,11},{11... | collective-permute-start | bytes 9224 | tf_op jit(solution)/shard_map/ppermute | solution.py:23
  65.4 5.8 %collective-permute-start.14 = (f32[10,1,256]{2,1,0:T(1,128)S(1)}, f32[10,1,256]{2,1,0:T(1,128)S(1)}, u32[]{:S(2)}, u32[]{:S(2)}) collective-permute-start(f32[10,1,256]{2,1,0:T(1,128)S(1)} %get-tuple-element.19), channel_id=1, source_target_pairs={{1,0},{2,1},{3,2},{4,3},{5,4},{6,5},{7,6},{9,8},{10,9},{11,10},{12... | collective-permute-start | bytes 30728 | tf_op jit(solution)/shard_map/ppermute | solution.py:26
  67.3 4.4 %collective-permute-start.15 = (f32[10,1,256]{2,1,0:T(1,128)S(1)}, f32[10,1,256]{2,1,0:T(1,128)S(1)}, u32[]{:S(2)}, u32[]{:S(2)}) collective-permute-start(f32[10,1,256]{2,1,0:T(1,128)S(1)} %get-tuple-element.18), channel_id=1, source_target_pairs={{0,1},{1,2},{2,3},{3,4},{4,5},{5,6},{6,7},{8,9},{9,10},{10,11},{11... | collective-permute-start | bytes 30728 | tf_op jit(solution)/shard_map/ppermute | solution.py:23
  73.9 14.9 %collective-permute-start.20 = (f32[1,32,128]{2,1,0:T(8,128)S(1)}, f32[1,32,128]{2,1,0:T(8,128)S(1)}, u32[]{:S(2)}, u32[]{:S(2)}) collective-permute-start(f32[1,32,128]{2,1,0:T(8,128)S(1)} %get-tuple-element.43), channel_id=1, source_target_pairs={{8,0},{16,8},{24,16},{32,24},{40,32},{48,40},{56,48},{64,56},{72,6... | collective-permute-start | bytes 49160 | tf_op jit(solution)/shard_map/ppermute | solution.py:26
  75.2 13.6 %collective-permute-start.21 = (f32[1,32,128]{2,1,0:T(8,128)S(1)}, f32[1,32,128]{2,1,0:T(8,128)S(1)}, u32[]{:S(2)}, u32[]{:S(2)}) collective-permute-start(f32[1,32,128]{2,1,0:T(8,128)S(1)} %get-tuple-element.42), channel_id=1, source_target_pairs={{0,8},{8,16},{16,24},{24,32},{32,40},{40,48},{48,56},{56,64},{64,7... | collective-permute-start | bytes 49160 | tf_op jit(solution)/shard_map/ppermute | solution.py:23
  81.1 23.5 %collective-permute-start.28 = (f32[1,16,64]{2,1,0:T(8,128)S(1)}, f32[1,16,64]{2,1,0:T(8,128)S(1)}, u32[]{:S(2)}, u32[]{:S(2)}) collective-permute-start(f32[1,16,64]{2,1,0:T(8,128)S(1)} %get-tuple-element.57), channel_id=1, source_target_pairs={{8,0},{16,8},{24,16},{32,24},{40,32},{48,40},{56,48},{64,56},{72,6... | collective-permute-start | bytes 12296 | tf_op jit(solution)/shard_map/ppermute | solution.py:26
  82.4 22.2 %collective-permute-start.29 = (f32[1,16,64]{2,1,0:T(8,128)S(1)}, f32[1,16,64]{2,1,0:T(8,128)S(1)}, u32[]{:S(2)}, u32[]{:S(2)}) collective-permute-start(f32[1,16,64]{2,1,0:T(8,128)S(1)} %get-tuple-element.56), channel_id=1, source_target_pairs={{0,8},{8,16},{16,24},{24,32},{32,40},{40,48},{48,56},{56,64},{64,7... | collective-permute-start | bytes 12296 | tf_op jit(solution)/shard_map/ppermute | solution.py:23
  88.8 6.8 %collective-permute-start.22 = (f32[6,1,128]{2,1,0:T(1,128)S(1)}, f32[6,1,128]{2,1,0:T(1,128)S(1)}, u32[]{:S(2)}, u32[]{:S(2)}) collective-permute-start(f32[6,1,128]{2,1,0:T(1,128)S(1)} %get-tuple-element.37), channel_id=1, source_target_pairs={{1,0},{2,1},{3,2},{4,3},{5,4},{6,5},{7,6},{9,8},{10,9},{11,10},{12... | collective-permute-start | bytes 9224 | tf_op jit(solution)/shard_map/ppermute | solution.py:26
  90.7 5.5 %collective-permute-start.23 = (f32[6,1,128]{2,1,0:T(1,128)S(1)}, f32[6,1,128]{2,1,0:T(1,128)S(1)}, u32[]{:S(2)}, u32[]{:S(2)}) collective-permute-start(f32[6,1,128]{2,1,0:T(1,128)S(1)} %get-tuple-element.36), channel_id=1, source_target_pairs={{0,1},{1,2},{2,3},{3,4},{4,5},{5,6},{6,7},{8,9},{9,10},{10,11},{11... | collective-permute-start | bytes 9224 | tf_op jit(solution)/shard_map/ppermute | solution.py:23
  96.5 55.5 %copy-start.4 = (f32[4,32,128]{2,1,0:T(8,128)}, f32[4,32,128]{2,1,0:T(8,128)S(1)}, u32[]{:S(2)}) copy-start(f32[4,32,128]{2,1,0:T(8,128)S(1)} %fusion.243) | copy-start | bytes 196612
  96.6 14.5 %collective-permute-start.24 = (f32[1,32,128]{2,1,0:T(8,128)S(1)}, f32[1,32,128]{2,1,0:T(8,128)S(1)}, u32[]{:S(2)}, u32[]{:S(2)}) collective-permute-start(f32[1,32,128]{2,1,0:T(8,128)S(1)} %get-tuple-element.41), channel_id=1, source_target_pairs={{8,0},{16,8},{24,16},{32,24},{40,32},{48,40},{56,48},{64,56},{72,6... | collective-permute-start | bytes 49160 | tf_op jit(solution)/shard_map/ppermute | solution.py:26
  97.9 13.2 %collective-permute-start.25 = (f32[1,32,128]{2,1,0:T(8,128)S(1)}, f32[1,32,128]{2,1,0:T(8,128)S(1)}, u32[]{:S(2)}, u32[]{:S(2)}) collective-permute-start(f32[1,32,128]{2,1,0:T(8,128)S(1)} %get-tuple-element.40), channel_id=1, source_target_pairs={{0,8},{8,16},{16,24},{24,32},{32,40},{40,48},{48,56},{56,64},{64,7... | collective-permute-start | bytes 49160 | tf_op jit(solution)/shard_map/ppermute | solution.py:23
  104.6 12.0 %collective-permute-start.30 = (f32[4,1,64]{2,1,0:T(1,128)S(1)}, f32[4,1,64]{2,1,0:T(1,128)S(1)}, u32[]{:S(2)}, u32[]{:S(2)}) collective-permute-start(f32[4,1,64]{2,1,0:T(1,128)S(1)} %get-tuple-element.51), channel_id=1, source_target_pairs={{1,0},{2,1},{3,2},{4,3},{5,4},{6,5},{7,6},{9,8},{10,9},{11,10},{12... | collective-permute-start | bytes 3080 | tf_op jit(solution)/shard_map/ppermute | solution.py:26
  106.6 10.1 %collective-permute-start.31 = (f32[4,1,64]{2,1,0:T(1,128)S(1)}, f32[4,1,64]{2,1,0:T(1,128)S(1)}, u32[]{:S(2)}, u32[]{:S(2)}) collective-permute-start(f32[4,1,64]{2,1,0:T(1,128)S(1)} %get-tuple-element.50), channel_id=1, source_target_pairs={{0,1},{1,2},{2,3},{3,4},{4,5},{5,6},{6,7},{8,9},{9,10},{10,11},{11... | collective-permute-start | bytes 3080 | tf_op jit(solution)/shard_map/ppermute | solution.py:23
  111.1 5.7 %collective-permute-start.26 = (f32[6,1,128]{2,1,0:T(1,128)S(1)}, f32[6,1,128]{2,1,0:T(1,128)S(1)}, u32[]{:S(2)}, u32[]{:S(2)}) collective-permute-start(f32[6,1,128]{2,1,0:T(1,128)S(1)} %get-tuple-element.35), channel_id=1, source_target_pairs={{1,0},{2,1},{3,2},{4,3},{5,4},{6,5},{7,6},{9,8},{10,9},{11,10},{12... | collective-permute-start | bytes 9224 | tf_op jit(solution)/shard_map/ppermute | solution.py:26
  113.0 4.4 %collective-permute-start.27 = (f32[6,1,128]{2,1,0:T(1,128)S(1)}, f32[6,1,128]{2,1,0:T(1,128)S(1)}, u32[]{:S(2)}, u32[]{:S(2)}) collective-permute-start(f32[6,1,128]{2,1,0:T(1,128)S(1)} %get-tuple-element.34), channel_id=1, source_target_pairs={{0,1},{1,2},{2,3},{3,4},{4,5},{5,6},{6,7},{8,9},{9,10},{10,11},{11... | collective-permute-start | bytes 9224 | tf_op jit(solution)/shard_map/ppermute | solution.py:23
  118.0 7.7 %collective-permute-start.32 = (f32[1,16,64]{2,1,0:T(8,128)S(1)}, f32[1,16,64]{2,1,0:T(8,128)S(1)}, u32[]{:S(2)}, u32[]{:S(2)}) collective-permute-start(f32[1,16,64]{2,1,0:T(8,128)S(1)} %get-tuple-element.55), channel_id=1, source_target_pairs={{8,0},{16,8},{24,16},{32,24},{40,32},{48,40},{56,48},{64,56},{72,6... | collective-permute-start | bytes 12296 | tf_op jit(solution)/shard_map/ppermute | solution.py:26
  119.3 7.2 %collective-permute-start.33 = (f32[1,16,64]{2,1,0:T(8,128)S(1)}, f32[1,16,64]{2,1,0:T(8,128)S(1)}, u32[]{:S(2)}, u32[]{:S(2)}) collective-permute-start(f32[1,16,64]{2,1,0:T(8,128)S(1)} %get-tuple-element.54), channel_id=1, source_target_pairs={{0,8},{8,16},{16,24},{24,32},{32,40},{40,48},{48,56},{56,64},{64,7... | collective-permute-start | bytes 12296 | tf_op jit(solution)/shard_map/ppermute | solution.py:23
  126.5 25.4 %collective-permute-start.34 = (f32[4,1,64]{2,1,0:T(1,128)S(1)}, f32[4,1,64]{2,1,0:T(1,128)S(1)}, u32[]{:S(2)}, u32[]{:S(2)}) collective-permute-start(f32[4,1,64]{2,1,0:T(1,128)S(1)} %get-tuple-element.49), channel_id=1, source_target_pairs={{1,0},{2,1},{3,2},{4,3},{5,4},{6,5},{7,6},{9,8},{10,9},{11,10},{12... | collective-permute-start | bytes 3080 | tf_op jit(solution)/shard_map/ppermute | solution.py:26
  128.4 23.5 %collective-permute-start.35 = (f32[4,1,64]{2,1,0:T(1,128)S(1)}, f32[4,1,64]{2,1,0:T(1,128)S(1)}, u32[]{:S(2)}, u32[]{:S(2)}) collective-permute-start(f32[4,1,64]{2,1,0:T(1,128)S(1)} %get-tuple-element.48), channel_id=1, source_target_pairs={{0,1},{1,2},{2,3},{3,4},{4,5},{5,6},{6,7},{8,9},{9,10},{10,11},{11... | collective-permute-start | bytes 3080 | tf_op jit(solution)/shard_map/ppermute | solution.py:23
  134.4 30.4 %all-to-all-start = ((f32[128,1,256]{2,1,0:T(1,128)}), f32[128,1,256]{2,1,0:T(1,128)S(1)}, u32[]{:S(2)}, u32[]{:S(2)}) async-start(f32[128,1,256]{2,1,0:T(1,128)} %stack.3), calls=%async_computation | async-start | bytes 262144 | tf_op jit(solution)/shard_map/all_to_all | solution.py:123
  152.1 57.2 %copy-start.5 = (f32[2,16,64]{2,1,0:T(8,128)}, f32[2,16,64]{2,1,0:T(8,128)S(1)}, u32[]{:S(2)}) copy-start(f32[2,16,64]{2,1,0:T(8,128)S(1)} %fusion.296) | copy-start | bytes 24580
  152.1 5.3 %collective-permute-start.36 = (f32[1,16,64]{2,1,0:T(8,128)S(1)}, f32[1,16,64]{2,1,0:T(8,128)S(1)}, u32[]{:S(2)}, u32[]{:S(2)}) collective-permute-start(f32[1,16,64]{2,1,0:T(8,128)S(1)} %get-tuple-element.53), channel_id=1, source_target_pairs={{8,0},{16,8},{24,16},{32,24},{40,32},{48,40},{56,48},{64,56},{72,6... | collective-permute-start | bytes 12296 | tf_op jit(solution)/shard_map/ppermute | solution.py:26
  153.4 4.8 %collective-permute-start.37 = (f32[1,16,64]{2,1,0:T(8,128)S(1)}, f32[1,16,64]{2,1,0:T(8,128)S(1)}, u32[]{:S(2)}, u32[]{:S(2)}) collective-permute-start(f32[1,16,64]{2,1,0:T(8,128)S(1)} %get-tuple-element.52), channel_id=1, source_target_pairs={{0,8},{8,16},{16,24},{24,32},{32,40},{40,48},{48,56},{56,64},{64,7... | collective-permute-start | bytes 12296 | tf_op jit(solution)/shard_map/ppermute | solution.py:23
  158.2 7.1 %collective-permute-start.38 = (f32[4,1,64]{2,1,0:T(1,128)S(1)}, f32[4,1,64]{2,1,0:T(1,128)S(1)}, u32[]{:S(2)}, u32[]{:S(2)}) collective-permute-start(f32[4,1,64]{2,1,0:T(1,128)S(1)} %get-tuple-element.47), channel_id=1, source_target_pairs={{1,0},{2,1},{3,2},{4,3},{5,4},{6,5},{7,6},{9,8},{10,9},{11,10},{12... | collective-permute-start | bytes 3080 | tf_op jit(solution)/shard_map/ppermute | solution.py:26
  162.3 3.2 %collective-permute-start.39 = (f32[4,1,64]{2,1,0:T(1,128)S(1)}, f32[4,1,64]{2,1,0:T(1,128)S(1)}, u32[]{:S(2)}, u32[]{:S(2)}) collective-permute-start(f32[4,1,64]{2,1,0:T(1,128)S(1)} %get-tuple-element.46), channel_id=1, source_target_pairs={{0,1},{1,2},{2,3},{3,4},{4,5},{5,6},{6,7},{8,9},{9,10},{10,11},{11... | collective-permute-start | bytes 3080 | tf_op jit(solution)/shard_map/ppermute | solution.py:23
